TPU v7x, 256 devices: a whole 4x4x8 slice. The times are simulated.
256 devices in a mesh: wide: 32 (over z, x), narrow: 8 (over y, core).
Axes of the slice: x: 4, y: 4, z: 8, core: 2. Of those that a mesh axis runs over, the one named last changes fastest.
Arguments:
- hidden_in: bfloat16 [64, 8192], P(None, 'wide'), may hold values from -6 to 6
- attn_gain: bfloat16 [8192], P('wide'), may hold values from 0.099609375 to 1.8984375
- qkv_weight: bfloat16 [8192, 8, 10, 128], P('wide', 'narrow'), may hold values from -2 to 2
- qkv_bias: bfloat16 [8, 10, 128], P('narrow'), may hold values from -3 to 3
- cache_keys: bfloat16 [64, 8, 4096, 128], P('wide', 'narrow'), may hold values from -256 to 256
- cache_values: bfloat16 [64, 8, 4096, 128], P('wide', 'narrow'), may hold values from -10 to 10
- positions: int32 [64, 3, 4096], P('wide'), may hold values from 0 to 4095
- lengths: int32 [64], P('wide'), may hold values from 512 to 4095, as said below
- out_weight: bfloat16 [8192, 8192], P('narrow', 'wide'), may hold values from -0.0625 to 0.0625
- mlp_gain: bfloat16 [8192], P('wide'), may hold values from 0.099609375 to 1.8984375
- gate_up_weight: bfloat16 [8192, 2, 29568], P('wide', None, 'narrow'), may hold values from -0.0625 to 0.0625
- down_weight: bfloat16 [29568, 8192], P('narrow', 'wide'), may hold values from -0.03125 to 0.03125
Outputs:
- layer_out: bfloat16 [64, 8192], P(None, 'wide')
Inputs may be any that keep to these rules, and one draw needn't show every extreme that they name: Slots 0 to lengths[b] - 1 of request b are filled, the new token takes slot lengths[b], and some request has 4095.
All inputs are finite; a program needn't handle non-finite values.
Results may differ from a plain program's by a relative error of at most 0.01115.
The roundings to bfloat16 on the way count: a program that leaves them out, or rounds other values in their place, can miss the bound.
Values may be sent and summed in bfloat16 or wider, within the bound.
No kernel may reach another device: no remote copies, remote signals or barrier semaphores. Data moves between devices by JAX's collectives and lax.ppermute only.
A program may use at most 64 MiB of HBM per device.

v0:
```python
import math
import jax
import jax.numpy as jnp
from jax import lax
from jax.sharding import PartitionSpec as P

D = 8192
DH = 128
CACHE = 4096
norm_eps = 1e-06
rope_base = 1000000.0


def mrope_tables(position):
    half_width = DH // 2
    pair_index = jnp.arange(half_width)
    inv_freq = jnp.exp(pair_index.astype(jnp.float32) * (-2.0 * math.log(rope_base) / DH))
    component = (pair_index >= DH // 8).astype(jnp.int32) + (
        pair_index >= DH // 8 + 3 * DH // 16
    ).astype(jnp.int32)
    pos_float = position.astype(jnp.float32)
    chosen = jnp.where(
        component == 0,
        pos_float[..., 0, :, None],
        jnp.where(component == 1, pos_float[..., 1, :, None], pos_float[..., 2, :, None]),
    )
    angles = chosen * inv_freq
    return (jnp.cos(angles), jnp.sin(angles))


def rotate(values, cosine, sine_table):
    half_width = values.shape[-1] // 2
    leading = values[..., :half_width]
    trailing = values[..., half_width:]
    return jnp.concatenate(
        [leading * cosine - trailing * sine_table, trailing * cosine + leading * sine_table],
        axis=-1,
    )


def local(
    hidden_in,
    attn_gain,
    qkv_weight,
    qkv_bias,
    cache_keys,
    cache_values,
    positions,
    lengths,
    out_weight,
    mlp_gain,
    gate_up_weight,
    down_weight,
):
    score_scale = 1.0 / math.sqrt(DH)
    owned = lengths.shape[0]
    local_rows = hidden_in.shape[1]
    kv_local = qkv_weight.shape[1]
    slot_count = qkv_weight.shape[2]
    group_size = slot_count - 2
    width = kv_local * slot_count * DH
    inputs = hidden_in.astype(jnp.float32)
    local_squares = jnp.sum(inputs * inputs, axis=1)
    scaled = (inputs * attn_gain.astype(jnp.float32)).astype(jnp.bfloat16)
    weight_flat = qkv_weight.reshape(local_rows, width)
    partial = jnp.dot(scaled, weight_flat, preferred_element_type=jnp.float32)
    summed = lax.psum_scatter(
        jnp.concatenate([partial, local_squares[:, None]], axis=1),
        "wide",
        scatter_dimension=0,
        tiled=True,
    )
    inv_rms = 1.0 / jnp.sqrt(summed[:, width] / D + norm_eps)
    projected = inv_rms[:, None] * summed[:, :width] + qkv_bias.reshape(width).astype(jnp.float32)
    projected = projected.reshape(owned, kv_local, slot_count, DH)
    cosine, sine_table = mrope_tables(positions)
    keys_rot = rotate(cache_keys.astype(jnp.float32), cosine[:, None], sine_table[:, None]).astype(
        jnp.bfloat16
    )
    new_position = jnp.take_along_axis(positions, lengths[:, None, None], axis=2)
    cos_new, sin_new = mrope_tables(new_position)
    query = rotate(projected[:, :, :group_size], cos_new[:, None], sin_new[:, None]).astype(
        jnp.bfloat16
    )
    key_new = rotate(projected[:, :, group_size], cos_new, sin_new).astype(jnp.bfloat16)
    value_new = projected[:, :, group_size + 1].astype(jnp.bfloat16)
    scores = (
        jnp.einsum("rgjd,rgsd->rgjs", query, keys_rot, preferred_element_type=jnp.float32)
        * score_scale
    )
    own_score = (
        jnp.sum(query.astype(jnp.float32) * key_new.astype(jnp.float32)[:, :, None, :], axis=3)
        * score_scale
    )
    valid_slot = jnp.arange(CACHE)[None, None, None, :] < lengths[:, None, None, None]
    row_max = jnp.maximum(jnp.max(jnp.where(valid_slot, scores, -jnp.inf), axis=3), own_score)
    probabilities = jnp.where(valid_slot, jnp.exp(scores - row_max[..., None]), 0.0)
    own_prob = jnp.exp(own_score - row_max)
    totals = jnp.sum(probabilities, axis=3) + own_prob
    probs_rounded = probabilities.astype(jnp.bfloat16)
    own_rounded = own_prob.astype(jnp.bfloat16).astype(jnp.float32)
    weighted = jnp.einsum(
        "rgjs,rgsd->rgjd", probs_rounded, cache_values, preferred_element_type=jnp.float32
    )
    weighted = weighted + own_rounded[..., None] * value_new.astype(jnp.float32)[:, :, None, :]
    attended = (
        (weighted / totals[..., None])
        .astype(jnp.bfloat16)
        .reshape(owned, kv_local * group_size * DH)
    )
    head_partial = jnp.dot(
        lax.all_gather(attended, "wide", axis=0, tiled=True),
        out_weight,
        preferred_element_type=jnp.float32,
    )
    attn_out = lax.psum(head_partial, "narrow")
    residual = (inputs + attn_out).astype(jnp.bfloat16)
    resid_float = residual.astype(jnp.float32)
    resid_squares = jnp.sum(resid_float * resid_float, axis=1)
    scaled2 = (resid_float * mlp_gain.astype(jnp.float32)).astype(jnp.bfloat16)
    hidden_local = gate_up_weight.shape[2]
    gate_up_flat = gate_up_weight.reshape(local_rows, 2 * hidden_local)
    partial2 = jnp.dot(scaled2, gate_up_flat, preferred_element_type=jnp.float32)
    summed2 = lax.psum(jnp.concatenate([partial2, resid_squares[:, None]], axis=1), "wide")
    inv_rms2 = 1.0 / jnp.sqrt(summed2[:, 2 * hidden_local] / D + norm_eps)
    gate_up = summed2[:, : 2 * hidden_local] * inv_rms2[:, None]
    hidden = (jax.nn.silu(gate_up[:, :hidden_local]) * gate_up[:, hidden_local:]).astype(
        jnp.bfloat16
    )
    down_partial = jnp.dot(hidden, down_weight, preferred_element_type=jnp.float32)
    mlp_out = lax.psum(down_partial, "narrow")
    return (resid_float + mlp_out).astype(jnp.bfloat16)


def solution(mesh):
    in_specs = (
        P(None, "wide"),
        P("wide"),
        P("wide", "narrow", None, None),
        P("narrow", None, None),
        P("wide", "narrow", None, None),
        P("wide", "narrow", None, None),
        P("wide", None, None),
        P("wide"),
        P("narrow", "wide"),
        P("wide"),
        P("wide", None, "narrow"),
        P("narrow", "wide"),
    )
    out_specs = P(None, "wide")
    return jax.shard_map(local, mesh=mesh, in_specs=in_specs, out_specs=out_specs, check_vma=False)
```

profile of v0, /device:TPU:2, one launch (start us, length us, event | category | flops | bytes accessed | tf_op | source)
XLA Modules:
  0.0 506.0 jit_solution(6786295929845901364)
XLA Ops:
  6.5 1.0 fusion.28
  7.7 1.3 copy.24
  9.0 0.7 convert_element_type.170
  9.7 1.1 fusion.35
  10.8 0.8 pad_maximum_fusion.1
  11.7 2.7 copy.27
  14.5 3.8 bitcast_convert_fusion
  18.4 0.2 or_reduce_fusion
  18.6 1.4 gather_fusion
  20.1 0.2 slice_reduce_fusion.1
  20.3 0.1 fusion.61
  20.4 19.8 %fusion.7 = (bf16[2,4096,64]{2,1,0:T(8,128)(2,1)}, bf16[2,4096,64]{2,1,0:T(8,128)(2,1)}) fusion(f32[2,1,4096,128]{3,2,0,1:T(8,128)} %bitcast_convert_fusion, f32[64]{0:T(128)S(1)} %multiply_exponential_fusion, f32[2,4096]{1,0:T(2,128)S(1)} %get-tuple-element.17, f32[2,4096]{1,0:T(2,128)S(1)} %get-tuple-element.18, f32[2,4096]{1,0:T(2,128)S(1)} %get-tuple-element.16, ...), kind=kLoop, calls=%fused_computation.13 | loop fusion | flops 5767168 | bytes 6390144 | tf_op jit(solution)/shard_map/concatenate | solution.py:35
  40.4 0.6 dynamic-slice
  41.7 118.7 %all-reduce.12.cloned.1.call-done = f32[64,1281]{1,0:T(8,128)} async-done(((f32[64,1281]{1,0:T(8,128)}), f32[64,1281]{1,0:T(8,128)}) %all-reduce.12.cloned.1.call-update) | async-done | bytes 327952
  160.3 0.9 fusion.50
  161.2 0.9 fusion.42
  162.3 0.2 multiply_reduce_fusion
  162.5 3.6 select_reduce_fusion
  166.1 0.2 fusion.21
  166.3 0.4 fusion.15
  166.8 41.9 %all-gather = bf16[32,2,1024]{2,1,0:T(2,128)(2,1)S(1)} all-gather(bf16[1,2,1024]{2,1,0:T(2,128)(2,1)S(1)} %reshape.653), channel_id=1, replica_groups=mesh['wide'=32,'narrow'=8] {'wide'}, dimensions={0}, use_global_device_ids=true | all-gather | bytes 135168 | tf_op jit(solution)/shard_map/all_gather | solution.py:112
  208.7 0.8 fusion.62
  209.6 63.7 %all-reduce.6.cloned.1.call-done = f32[64,256]{1,0:T(8,128)} async-done(((f32[64,256]{1,0:T(8,128)}), f32[64,256]{1,0:T(8,128)}) %all-reduce.6.cloned.1.call-update) | async-done | bytes 65552 | tf_op jit(solution)/shard_map/psum | solution.py:116
  273.3 0.9 fusion.31
  274.3 3.4 fusion.33
  277.7 1.4 pad_maximum_fusion
  279.1 151.0 %all-reduce.8.cloned.1.call-done = f32[64,7393]{1,0:T(8,128)} async-done(((f32[64,7393]{1,0:T(8,128)}), f32[64,7393]{1,0:T(8,128)}) %all-reduce.8.cloned.1.call-update) | async-done | bytes 1892624 | tf_op jit(solution)/shard_map/psum | solution.py:124
  430.2 1.1 fusion.39
  431.2 1.7 slice_multiply_fusion
  433.0 1.2 fusion.19
  434.2 63.8 %all-reduce.10.cloned.1.call-done = f32[64,256]{1,0:T(8,128)} async-done(((f32[64,256]{1,0:T(8,128)}), f32[64,256]{1,0:T(8,128)}) %all-reduce.10.cloned.1.call-update) | async-done | bytes 65552 | tf_op jit(solution)/shard_map/psum | solution.py:131
  498.0 1.5 fusion.32
  (53 shorter events, 1.3 us)
Async XLA Ops:
  6.5 159.8 %copy-start = (bf16[2,1,4096,128]{3,2,1,0:T(8,128)(2,1)S(1)}, bf16[2,1,4096,128]{3,2,1,0:T(8,128)(2,1)}, u32[]{:S(2)}) copy-start(bf16[2,1,4096,128]{3,2,1,0:T(8,128)(2,1)} %param.17) | copy-start | bytes 6291460
  6.5 5.1 %copy-start.2 = (s32[2,3,4096]{2,0,1:T(2,128)S(1)}, s32[2,3,4096]{2,0,1:T(2,128)}, u32[]{:S(2)}) copy-start(s32[2,3,4096]{2,0,1:T(2,128)} %param.18) | copy-start | bytes 294916
  6.5 153.8 %all-reduce.12.cloned.1.call-start = ((), (), s32[]{:S(2)}) async-start(), calls=%async_computation.3 | async-start | bytes 720896
  11.6 261.7 %all-reduce.6.cloned.1.call-start = ((), (), s32[]{:S(2)}) async-start(), calls=%async_computation | async-start | bytes 131072 | tf_op jit(solution)/shard_map/psum | solution.py:116
  11.7 2.7 copy-start.5
  20.4 20.0 %copy-start.8 = (u32[256]{0:T(256)S(1)}, u32[256]{0:T(256)}, u32[]{:S(2)}) copy-start(u32[256]{0:T(256)} %constant.64) | copy-start | bytes 3076
  20.4 21.2 %copy-start.4 = (bf16[1,10,128]{2,1,0:T(8,128)(2,1)S(1)}, bf16[1,10,128]{2,1,0:T(8,128)(2,1)}, u32[]{:S(2)}) copy-start(bf16[1,10,128]{2,1,0:T(8,128)(2,1)} %param.15) | copy-start | bytes 7684
  166.0 42.6 %copy-start.1 = (bf16[1024,256]{1,0:T(8,128)(2,1)S(1)}, bf16[1024,256]{1,0:T(8,128)(2,1)}, u32[]{:S(2)}) copy-start(bf16[1024,256]{1,0:T(8,128)(2,1)} %param.20) | copy-start | bytes 1572868
  166.0 43.5 %copy-start.7 = (bf16[256]{0:T(256)(128)(2,1)S(1)}, bf16[256]{0:T(256)(128)(2,1)}, u32[]{:S(2)}) copy-start(bf16[256]{0:T(256)(128)(2,1)} %param.21) | copy-start | bytes 1540
  166.0 107.2 %copy-start.3 = (bf16[64,256]{1,0:T(8,128)(2,1)S(1)}, bf16[64,256]{1,0:T(8,128)(2,1)}, u32[]{:S(2)}) copy-start(bf16[64,256]{1,0:T(8,128)(2,1)} %param.12) | copy-start | bytes 98308
  209.5 220.6 %all-reduce.8.cloned.1.call-start = ((), (), s32[]{:S(2)}) async-start(), calls=%async_computation.1 | async-start | bytes 3801088 | tf_op jit(solution)/shard_map/psum | solution.py:124
  279.1 218.9 %all-reduce.10.cloned.1.call-start = ((), (), s32[]{:S(2)}) async-start(), calls=%async_computation.2 | async-start | bytes 131072 | tf_op jit(solution)/shard_map/psum | solution.py:131
  430.2 2.8 copy-start.6
Sparse Core Ops, SparseCore 0:
  11.7 148.5 all-reduce.11
  209.6 63.5 all-reduce.5
  279.2 150.9 all-reduce.7
  434.3 63.6 all-reduce.9
where the time goes:
time: 507 us; the launch traced here: 506 us
  waiting for transfers between devices  397 us (78%)
  blocking collectives  41.9 us (8%)
  other arithmetic  35.6 us (7%)
  between operations  14 us (3%)
  matrix products  10.4 us (2%)
  local copies, waits for them, and re-layouts  6.65 us (1%)
    psum x1, waiting for transfers between devices, local(): lax.psum(jnp.concatenate([partial2, resid_squares[:, None]], axis=1), 'wi...  151 us
    unnamed x5, waiting for transfers between devices  119 us
    psum x1, waiting for transfers between devices, local(): mlp_out = lax.psum(down_partial, 'narrow')  63.8 us
    psum x1, waiting for transfers between devices, local(): attn_out = lax.psum(head_partial, 'narrow')  63.7 us
    all_gather x1, blocking collectives, local(): lax.all_gather(attended, 'wide', axis=0, tiled=True)  41.9 us
    concatenate x2, other arithmetic, rotate(): jnp.concatenate([leading * cosine - trailing * sine_table, trailing * cos...  19.8 us
  transfers between devices with their start and end apart: 4, of which 4 were waited for; matrix products, arithmetic and copies ran while one was open for 6% of the time, Pallas kernels for 0%

commit v1 on v0

--- a/solution.py
+++ b/solution.py
@@ -9,6 +9,7 @@
 CACHE = 4096
 norm_eps = 1e-06
 rope_base = 1000000.0
+_assign_rates = lambda block_here: lax.all_gather(block_here, "narrow").sum(axis=0)
 
 
 def mrope_tables(position):
@@ -113,7 +114,7 @@
         out_weight,
         preferred_element_type=jnp.float32,
     )
-    attn_out = lax.psum(head_partial, "narrow")
+    attn_out = _assign_rates(head_partial)
     residual = (inputs + attn_out).astype(jnp.bfloat16)
     resid_float = residual.astype(jnp.float32)
     resid_squares = jnp.sum(resid_float * resid_float, axis=1)

time: 507 us -> 454 us (0.90)
  waiting for transfers between devices: 397 us -> 333 us
  blocking collectives: 41.9 us -> 55.3 us
    psum x1 -> x0, waiting for transfers between devices: 63.7 us -> none  [local(): attn_out = lax.psum(head_partial, 'narrow')]
    all_gather x0 -> x1, blocking collectives: none -> 13.4 us  [lax.all_gather(block_here, 'narrow').sum(axis=0)]
    unnamed x5 -> x4, waiting for transfers between devices: 119 us -> 119 us
  transfers between devices with their start and end apart: 4 -> 3, of which waited for: 4 -> 3; matrix products, arithmetic and copies ran while one was open for 6% -> 6% of each run, Pallas kernels for 0% -> 0%
where the time goes in v1:
time: 454 us; the launch traced here: 453 us
  waiting for transfers between devices  333 us (73%)
  blocking collectives  55.3 us (12%)
  other arithmetic  34.8 us (8%)
  between operations  14 us (3%)
  matrix products  9.82 us (2%)
  local copies, waits for them, and re-layouts  6.65 us (1%)
    psum x1, waiting for transfers between devices, local(): lax.psum(jnp.concatenate([partial2, resid_squares[:, None]], axis=1), 'wi...  150 us
    unnamed x4, waiting for transfers between devices  119 us
    psum x1, waiting for transfers between devices, local(): mlp_out = lax.psum(down_partial, 'narrow')  63.8 us
    all_gather x1, blocking collectives, local(): lax.all_gather(attended, 'wide', axis=0, tiled=True)  41.9 us
    concatenate x2, other arithmetic, rotate(): jnp.concatenate([leading * cosine - trailing * sine_table, trailing * cos...  19.8 us
    all_gather x1, blocking collectives, lax.all_gather(block_here, 'narrow').sum(axis=0)  13.4 us
  transfers between devices with their start and end apart: 3, of which 3 were waited for; matrix products, arithmetic and copies ran while one was open for 6% of the time, Pallas kernels for 0%

profile of v1, /device:TPU:2, one launch (start us, length us, event | category | flops | bytes accessed | tf_op | source)
XLA Modules:
  0.0 453.3 jit_solution(2820658217397555160)
XLA Ops:
  6.5 1.0 fusion.28
  7.7 1.3 copy.24
  9.0 0.7 convert_element_type.170
  9.7 1.1 fusion.35
  10.8 0.8 pad_maximum_fusion.1
  11.7 2.7 copy.27
  14.5 3.8 bitcast_convert_fusion
  18.4 0.2 or_reduce_fusion
  18.6 1.4 gather_fusion
  20.1 0.2 slice_reduce_fusion.1
  20.3 0.1 fusion.61
  20.5 19.8 %fusion.7 = (bf16[2,4096,64]{2,1,0:T(8,128)(2,1)}, bf16[2,4096,64]{2,1,0:T(8,128)(2,1)}) fusion(f32[2,1,4096,128]{3,2,0,1:T(8,128)} %bitcast_convert_fusion, f32[64]{0:T(128)S(1)} %multiply_exponential_fusion, f32[2,4096]{1,0:T(2,128)S(1)} %get-tuple-element.17, f32[2,4096]{1,0:T(2,128)S(1)} %get-tuple-element.18, f32[2,4096]{1,0:T(2,128)S(1)} %get-tuple-element.16, ...), kind=kLoop, calls=%fused_computation.13 | loop fusion | flops 5767168 | bytes 6390144 | tf_op jit(solution)/shard_map/concatenate | solution.py:36
  40.4 0.6 dynamic-slice
  41.7 118.6 %all-reduce.9.cloned.1.call-done = f32[64,1281]{1,0:T(8,128)} async-done(((f32[64,1281]{1,0:T(8,128)}), f32[64,1281]{1,0:T(8,128)}) %all-reduce.9.cloned.1.call-update) | async-done | bytes 327952
  160.3 0.9 fusion.50
  161.2 0.9 fusion.42
  162.3 0.2 multiply_reduce_fusion
  162.5 3.6 select_reduce_fusion
  166.0 0.2 fusion.21
  166.3 0.4 fusion.15
  166.8 41.9 %all-gather.1 = bf16[32,2,1024]{2,1,0:T(2,128)(2,1)S(1)} all-gather(bf16[1,2,1024]{2,1,0:T(2,128)(2,1)S(1)} %reshape.654), channel_id=1, replica_groups=mesh['wide'=32,'narrow'=8] {'wide'}, dimensions={0}, use_global_device_ids=true | all-gather | bytes 135168 | tf_op jit(solution)/shard_map/all_gather | solution.py:113
  208.7 0.2 fusion.62
  208.9 13.4 %all-gather = f32[512,256]{1,0:T(8,128)S(1)} all-gather(f32[64,256]{1,0:T(8,128)S(1)} %fusion.62), channel_id=2, replica_groups=mesh['wide'=32,'narrow'=8] {'narrow'}, dimensions={0}, use_global_device_ids=true | all-gather | bytes 589824 | tf_op jit(solution)/shard_map/all_gather | solution.py:12
  222.4 0.1 fusion.31
  222.6 3.3 fusion.33
  225.9 1.4 pad_maximum_fusion
  227.4 150.1 %all-reduce.5.cloned.1.call-done = f32[64,7393]{1,0:T(8,128)} async-done(((f32[64,7393]{1,0:T(8,128)}), f32[64,7393]{1,0:T(8,128)}) %all-reduce.5.cloned.1.call-update) | async-done | bytes 1892624 | tf_op jit(solution)/shard_map/psum | solution.py:125
  377.5 1.1 fusion.39
  378.6 1.7 slice_multiply_fusion
  380.3 1.2 fusion.19
  381.5 63.8 %all-reduce.7.cloned.1.call-done = f32[64,256]{1,0:T(8,128)} async-done(((f32[64,256]{1,0:T(8,128)}), f32[64,256]{1,0:T(8,128)}) %all-reduce.7.cloned.1.call-update) | async-done | bytes 65552 | tf_op jit(solution)/shard_map/psum | solution.py:132
  445.3 1.5 fusion.32
  (52 shorter events, 1.2 us)
Async XLA Ops:
  6.5 159.7 %copy-start = (bf16[2,1,4096,128]{3,2,1,0:T(8,128)(2,1)S(1)}, bf16[2,1,4096,128]{3,2,1,0:T(8,128)(2,1)}, u32[]{:S(2)}) copy-start(bf16[2,1,4096,128]{3,2,1,0:T(8,128)(2,1)} %param.17) | copy-start | bytes 6291460
  6.5 5.1 %copy-start.2 = (s32[2,3,4096]{2,0,1:T(2,128)S(1)}, s32[2,3,4096]{2,0,1:T(2,128)}, u32[]{:S(2)}) copy-start(s32[2,3,4096]{2,0,1:T(2,128)} %param.18) | copy-start | bytes 294916
  6.5 153.8 %all-reduce.9.cloned.1.call-start = ((), (), s32[]{:S(2)}) async-start(), calls=%async_computation.2 | async-start | bytes 720896
  11.6 365.9 %all-reduce.5.cloned.1.call-start = ((), (), s32[]{:S(2)}) async-start(), calls=%async_computation | async-start | bytes 3801088 | tf_op jit(solution)/shard_map/psum | solution.py:125
  11.7 2.7 copy-start.5
  20.4 20.0 %copy-start.7 = (bf16[256]{0:T(256)(128)(2,1)S(1)}, bf16[256]{0:T(256)(128)(2,1)}, u32[]{:S(2)}) copy-start(bf16[256]{0:T(256)(128)(2,1)} %param.21) | copy-start | bytes 1540
  20.4 20.0 %copy-start.8 = (u32[256]{0:T(256)S(1)}, u32[256]{0:T(256)}, u32[]{:S(2)}) copy-start(u32[256]{0:T(256)} %constant.64) | copy-start | bytes 3076
  20.4 21.2 %copy-start.4 = (bf16[1,10,128]{2,1,0:T(8,128)(2,1)S(1)}, bf16[1,10,128]{2,1,0:T(8,128)(2,1)}, u32[]{:S(2)}) copy-start(bf16[1,10,128]{2,1,0:T(8,128)(2,1)} %param.15) | copy-start | bytes 7684
  166.0 42.6 %copy-start.1 = (bf16[1024,256]{1,0:T(8,128)(2,1)S(1)}, bf16[1024,256]{1,0:T(8,128)(2,1)}, u32[]{:S(2)}) copy-start(bf16[1024,256]{1,0:T(8,128)(2,1)} %param.20) | copy-start | bytes 1572868
  166.3 56.1 %copy-start.3 = (bf16[64,256]{1,0:T(8,128)(2,1)S(1)}, bf16[64,256]{1,0:T(8,128)(2,1)}, u32[]{:S(2)}) copy-start(bf16[64,256]{1,0:T(8,128)(2,1)} %param.12) | copy-start | bytes 98308
  227.3 218.0 %all-reduce.7.cloned.1.call-start = ((), (), s32[]{:S(2)}) async-start(), calls=%async_computation.1 | async-start | bytes 131072 | tf_op jit(solution)/shard_map/psum | solution.py:132
  377.5 2.8 copy-start.6
Sparse Core Ops, SparseCore 0:
  11.7 148.5 all-reduce.8
  227.5 149.9 all-reduce.4
  381.6 63.6 all-reduce.6
